TPU v7x, 128 devices: a whole 4x4x4 slice. The times are simulated.
128 devices in a mesh: req: 32 (over x, z, core), tp: 4 (over y).
Axes of the slice: x: 4, y: 4, z: 4, core: 2. Of those that a mesh axis runs over, the one named last changes fastest.
Arguments:
- hidden: bfloat16 [8192, 2048], P('req', 'tp'), may hold values from -45 to 45
- routes: int32 [8192, 2], P('req'), may hold values from 0 to 7, all different within a row; in each aligned block of 256 rows (0 to 255, 256 to 511, ...) at most 128 rows name the same one
- route_weights: float32 [8192, 2], P('req'), may hold values from 0.2 to 1
- pre_gain: float32 [2048], replicated, may hold values from 0.1 to 1.9
- out_gain: float32 [2048], P('tp'), may hold values from 0.1 to 1.9
- gate_weight: bfloat16 [32, 2048, 5632], P('req', None, 'tp'), as said below
- up_weight: bfloat16 [32, 2048, 5632], P('req', None, 'tp'), as said below
- down_weight: bfloat16 [32, 5632, 2048], P('req', 'tp'), as said below
Outputs:
- residual_out: bfloat16 [8192, 2048], P('req', 'tp')
- normed_out: bfloat16 [8192, 2048], P('req', 'tp')
Inputs may be any that keep to these rules, and one draw needn't show every extreme that they name: `routes`: each row names 2 different experts; in the rows of one index of req no expert is named by more than 128 rows, a bound that some block reaches. `gate_weight`: index r holds expert r % 8. `up_weight`: index r holds expert r % 8. `down_weight`: index r holds expert r % 8.
All inputs are finite; a program needn't handle non-finite values.
Results may differ from a plain program's by a relative error of at most 0.007.
Values may be sent and summed in bfloat16 or wider, within the bound.
No kernel may reach another device: no remote copies, remote signals or barrier semaphores. Data moves between devices by JAX's collectives and lax.ppermute only.
A program may use at most 128 MiB of HBM per device.

v0:
```python
import jax
import jax.numpy as jnp
from jax import lax
from jax.sharding import PartitionSpec as P

E = 8
CAP = 128
epsilon = 1e-05


def shards(hidden, routes, route_weights, pre_gain, out_gain, gate_weight, up_weight, down_weight):
    row_count, col_part = hidden.shape
    tp_count = lax.axis_size("tp")
    req_count = lax.axis_size("req")
    full_width = col_part * tp_count
    copies = req_count // E
    slot_count = CAP // copies
    stream = hidden.astype(jnp.float32)
    whole_rows = lax.all_gather(hidden, "tp", axis=1, tiled=True).astype(jnp.float32)
    meansq = jnp.sum(whole_rows * whole_rows, axis=1) / full_width
    normed_in = (whole_rows * lax.rsqrt(meansq + epsilon)[:, None] * pre_gain[None, :]).astype(
        jnp.bfloat16
    )
    send_cols = normed_in.shape[1]
    top = routes.shape[1]
    chosen = routes.reshape(-1)
    onehot = (chosen[:, None] == jnp.arange(E, dtype=jnp.int32)[None, :]).astype(jnp.int32)
    slot_rank = jnp.sum((jnp.cumsum(onehot, axis=0) - 1) * onehot, axis=1)
    dest = slot_rank % copies * E + chosen
    out_idx = dest * slot_count + slot_rank // copies
    out_pairs = out_idx.reshape(row_count, top)
    slot_ids = jnp.arange(req_count * slot_count, dtype=jnp.int32)
    dispatch = jnp.zeros((req_count * slot_count, row_count), jnp.bool_)
    for k in range(top):
        dispatch = dispatch | (slot_ids[:, None] == out_pairs[None, :, k])
    outgoing = jnp.dot(
        dispatch.astype(jnp.bfloat16), normed_in, preferred_element_type=jnp.float32
    ).astype(jnp.bfloat16)
    outgoing = outgoing.reshape(req_count, slot_count, send_cols)
    pieces = lax.all_to_all(outgoing, "req", split_axis=0, concat_axis=0, tiled=True)
    sources, items, widths = pieces.shape
    flat_rows = pieces.reshape(sources * items, widths)
    gate_val = jnp.dot(flat_rows, gate_weight[0], preferred_element_type=jnp.float32)
    up_val = jnp.dot(flat_rows, up_weight[0], preferred_element_type=jnp.float32)
    activ = (jax.nn.silu(gate_val) * up_val).astype(jnp.bfloat16)
    partial_out = jnp.dot(activ, down_weight[0], preferred_element_type=jnp.float32)
    partial_out = lax.optimization_barrier(partial_out.astype(jnp.bfloat16)).astype(jnp.float32)
    summed = lax.psum_scatter(
        partial_out.reshape(sources, items, widths).astype(jnp.bfloat16),
        "tp",
        scatter_dimension=2,
        tiled=True,
    )
    returned = lax.all_to_all(summed, "req", split_axis=0, concat_axis=0, tiled=True)
    returned = returned.reshape(req_count * slot_count, col_part)
    picked = returned[out_idx].reshape(row_count, top, col_part).astype(jnp.float32)
    mixed = jnp.sum(picked * route_weights[:, :, None], axis=1)
    total_stream = stream + mixed
    out_sums = lax.psum(jnp.sum(total_stream * total_stream, axis=1), "tp")
    normed_out = (
        total_stream * lax.rsqrt(out_sums / full_width + epsilon)[:, None] * out_gain[None, :]
    )
    return (total_stream.astype(jnp.bfloat16), normed_out.astype(jnp.bfloat16))


def solution(mesh):
    return jax.shard_map(
        shards,
        mesh=mesh,
        in_specs=(
            P("req", "tp"),
            P("req", None),
            P("req", None),
            P(),
            P("tp"),
            P("req", None, "tp"),
            P("req", None, "tp"),
            P("req", "tp", None),
        ),
        out_specs=(P("req", "tp"), P("req", "tp")),
        check_vma=False,
    )
```

profile of v0, /device:TPU:0, one launch (start us, length us, event | category | flops | bytes accessed | tf_op | source)
XLA Modules:
  0.0 217.9 jit_solution(11316550749932052494)
XLA Ops:
  7.2 0.0 all-gather.2.cloned.1.call-start
  7.2 0.7 all-gather.2.cloned.1.call-update
  7.9 0.0 reduce-scatter.2.cloned.1.call-start
  7.9 0.8 copy.27
  8.8 0.1 eq.62
  8.9 0.1 eq.58
  9.1 1.1 reduce-window.6
  10.2 0.2 slice_reduce_fusion
  10.5 0.1 fusion.27
  10.6 0.1 reduce_sum.41
  10.7 0.1 copy.29
  10.8 0.7 fusion.31
  11.5 24.6 %all-gather.2.cloned.1.call-done = bf16[256,2048]{1,0:T(8,128)(2,1)} async-done(((bf16[256,512]{1,0:T(8,128)(2,1)}), bf16[256,2048]{1,0:T(8,128)(2,1)}) %all-gather.2.cloned.1.call-update) | async-done | bytes 1048592 | tf_op jit(solution)/shard_map/all_gather | solution.py:19
  36.1 0.0 slice-start
  36.1 1.7 fusion.16
  37.8 0.0 slice-start.1
  37.8 2.7 %convolution_convert_fusion = bf16[1024,2048]{1,0:T(8,128)(2,1)S(1)} fusion(bf16[256,2048]{1,0:T(8,128)(2,1)} %all-gather.2.cloned.1.call-done, f32[2048]{0:T(1024)} %param.11, f32[256]{0:T(256)S(1)} %add_rsqrt_fusion.1, s32[256]{0:T(256)S(1)} %bitcast.40, s32[256]{0:T(256)S(1)} %bitcast.39), kind=kOutput, calls=%fused_computation.8 | convolution fusion | flops 1078722560 | bytes 5254144 | tf_op jit(solution)/shard_map/dot_general | solution.py:36
  40.6 57.5 %all_to_all.10 = bf16[32,32,2048]{2,1,0:T(8,128)(2,1)S(1)} all-to-all(bf16[32,32,2048]{2,1,0:T(8,128)(2,1)S(1)} %bitcast.33), channel_id=1, replica_groups=mesh['req'=32,'tp'=4] {'req'}, dimensions={0} | all-to-all | bytes 8388608 | tf_op jit(solution)/shard_map/all_to_all | solution.py:40
  98.1 0.0 copy-start
  98.1 2.1 copy-done
  100.2 0.0 slice-done
  100.2 0.0 slice-done.1
  100.2 8.4 %fusion.4 = f32[1024,1408]{1,0:T(8,128)} fusion(bf16[1024,2048]{1,0:T(8,128)(2,1)S(1)} %bitcast.36, bf16[1,2048,1408]{2,1,0:T(8,128)(2,1)S(1)} %bitcast.43), kind=kOutput, calls=%fused_computation.5 | convolution fusion | flops 5905580032 | bytes 15728640 | tf_op jit(solution)/shard_map/dot_general | solution.py:43
  108.6 20.6 %fusion.10 = bf16[1024,2048]{1,0:T(8,128)(2,1)} fusion(bf16[1,1408,2048]{2,1,0:T(8,128)(2,1)} %param.15, f32[1024,1408]{1,0:T(8,128)} %fusion.4, bf16[1024,2048]{1,0:T(8,128)(2,1)} %bitcast.37, bf16[1,2048,1408]{2,1,0:T(8,128)(2,1)} %param.14), kind=kOutput, calls=%fused_computation.9 | convolution fusion | flops 11821907968 | bytes 25690112 | tf_op jit(solution)/shard_map/dot_general | solution.py:46
  129.3 0.0 copy-start.2
  129.3 0.0 reduce-scatter.2.cloned.1.call-update
  129.3 0.0 copy-start.1
  129.3 0.0 copy-start.3
  129.3 44.1 %reduce-scatter.2.cloned.1.call-done = bf16[32,32,512]{2,1,0:T(8,128)(2,1)} async-done(((bf16[32,32,2048]{2,1,0:T(8,128)(2,1)}), bf16[32,32,512]{2,1,0:T(8,128)(2,1)}) %reduce-scatter.2.cloned.1.call-update) | async-done | bytes 1048592 | tf_op jit(solution)/shard_map/reduce_scatter | solution.py:48
  173.4 7.4 %all-to-all-start.1 = ((bf16[32,32,512]{2,1,0:T(8,128)(2,1)}), bf16[32,32,512]{2,1,0:T(8,128)(2,1)S(1)}, u32[]{:S(2)}, u32[]{:S(2)}) async-start(bf16[32,32,512]{2,1,0:T(8,128)(2,1)} %reduce-scatter.2.cloned.1.call-done), calls=%async_computation.2 | async-start | bytes 2097152 | tf_op jit(solution)/shard_map/all_to_all | solution.py:54
  180.8 0.1 reshape.153
  181.0 0.0 copy-done.2
  181.0 0.1 copy.34
  181.2 16.3 %all-to-all-done.1 = bf16[32,32,512]{2,1,0:T(8,128)(2,1)S(1)} async-done(((bf16[32,32,512]{2,1,0:T(8,128)(2,1)}), bf16[32,32,512]{2,1,0:T(8,128)(2,1)S(1)}, u32[]{:S(2)}, u32[]{:S(2)}) %all-to-all-start.1) | async-done | bytes 1048608 | tf_op jit(solution)/shard_map/all_to_all | solution.py:54
  197.5 2.0 gather_fusion
  199.4 0.7 reshape.154
  200.1 1.3 multiply_reduce_fusion
  201.4 0.0 copy-done.1
  201.4 0.2 multiply_reduce_fusion.1
  201.6 8.6 %psum.7 = f32[256]{0:T(256)S(1)} all-reduce(f32[256]{0:T(256)S(1)} %multiply_reduce_fusion.1), channel_id=1, replica_groups=mesh['req'=32,'tp'=4] {'tp'}, use_global_device_ids=true, to_apply=%region_7.8 | all-reduce | flops 256 | bytes 2048 | tf_op jit(solution)/shard_map/psum | solution.py:59
  210.2 0.0 copy-done.3
  210.2 0.9 multiply_convert_fusion.1
  (9 shorter events, 0.1 us)
Async XLA Ops:
  7.2 29.0 %all-gather.2.cloned.1.call-start = ((), (), s32[]{:S(2)}) async-start(), calls=%async_computation.3 | async-start | bytes 1310720 | tf_op jit(solution)/shard_map/all_gather | solution.py:19
  7.9 165.5 %reduce-scatter.2.cloned.1.call-start = ((), (), s32[]{:S(2)}) async-start(), calls=%async_computation.4 | async-start | bytes 5242880 | tf_op jit(solution)/shard_map/reduce_scatter | solution.py:48
  36.1 64.1 %slice-start = ((s8[5767168]{0:T(1024)(128)(4,1)}), s8[4194304]{0:T(1024)(128)(4,1)S(1)}, s32[]{:S(2)}) async-start(s8[5767168]{0:T(1024)(128)(4,1)} %bitcast.42), calls=%async_computation.5 | async-start | bytes 8388608
  37.8 62.4 %slice-start.1 = ((s8[5767168]{0:T(1024)(128)(4,1)}), s8[1572864]{0:T(1024)(128)(4,1)S(1)}, s32[]{:S(2)}) async-start(s8[5767168]{0:T(1024)(128)(4,1)} %bitcast.42), calls=%async_computation.6 | async-start | bytes 3145728
  98.1 2.1 copy-start
  129.3 51.7 %copy-start.2 = (f32[256,2]{0,1:T(2,128)S(1)}, f32[256,2]{0,1:T(2,128)}, u32[]{:S(2)}) copy-start(f32[256,2]{0,1:T(2,128)} %param.10) | copy-start | bytes 6148
  129.3 72.1 %copy-start.1 = (bf16[256,512]{1,0:T(8,128)(2,1)S(1)}, bf16[256,512]{1,0:T(8,128)(2,1)}, u32[]{:S(2)}) copy-start(bf16[256,512]{1,0:T(8,128)(2,1)} %param.8) | copy-start | bytes 786436
  129.3 80.9 %copy-start.3 = (f32[512]{0:T(512)S(1)}, f32[512]{0:T(512)}, u32[]{:S(2)}) copy-start(f32[512]{0:T(512)} %param.12) | copy-start | bytes 6148
  173.4 24.1 %all-to-all-start.1 = ((bf16[32,32,512]{2,1,0:T(8,128)(2,1)}), bf16[32,32,512]{2,1,0:T(8,128)(2,1)S(1)}, u32[]{:S(2)}, u32[]{:S(2)}) async-start(bf16[32,32,512]{2,1,0:T(8,128)(2,1)} %reduce-scatter.2.cloned.1.call-done), calls=%async_computation.2 | async-start | bytes 2097152 | tf_op jit(solution)/shard_map/all_to_all | solution.py:54
Sparse Core Ops, SparseCore 0:
  9.7 26.4 all-gather.1
  129.4 43.9 reduce-scatter.1
where the time goes:
time: 218 us
  waiting for transfers between devices  85.7 us (39%)
  blocking collectives  66.1 us (30%)
  matrix products  31.8 us (15%)
  between operations  14.2 us (7%)
  starting transfers between devices  7.49 us (3%)
  local copies, waits for them, and re-layouts  6.53 us (3%)
  other arithmetic  6.04 us (3%)
    all_to_all x1, blocking collectives, shards(): lax.all_to_all(outgoing, 'req', split_axis=0, concat_axis=0, tiled=True)  57.5 us
    reduce_scatter x1, waiting for transfers between devices, shards(): lax.psum_scatter(partial_out.reshape(sources, items, widths).astype(jnp.b...  44.1 us
    all_gather x1, waiting for transfers between devices, shards(): lax.all_gather(hidden, 'tp', axis=1, tiled=True).astype(jnp.float32)  24.6 us
    dot_general x1, matrix products, shards(): jnp.dot(activ, down_weight[0], preferred_element_type=jnp.float32)  20.6 us
    all_to_all x1, waiting for transfers between devices, shards(): lax.all_to_all(summed, 'req', split_axis=0, concat_axis=0, tiled=True)  16.3 us
    psum x1, blocking collectives, shards(): out_sums = lax.psum(jnp.sum(total_stream * total_stream, axis=1), 'tp')  8.58 us
    dot_general x1, matrix products, shards(): jnp.dot(flat_rows, gate_weight[0], preferred_element_type=jnp.float32)  8.44 us
    all_to_all x1, starting transfers between devices, shards(): lax.all_to_all(summed, 'req', split_axis=0, concat_axis=0, tiled=True)  7.41 us
  transfers between devices with their start and end apart: 3, of which 3 were waited for; matrix products, arithmetic and copies ran while one was open for 2% of the time, Pallas kernels for 0%

commit v1 on v0

--- a/solution.py
+++ b/solution.py
@@ -8,6 +8,33 @@
 epsilon = 1e-05
 
 
+def bring_space(x_part, array_dim):
+    link_axis = "tp"
+    view_out = lax.axis_size(link_axis)
+    spare, y1, outer = (view_out, lax.axis_index(link_axis), x_part.shape[array_dim])
+    f_now = jnp.zeros(
+        [idx * spare if dd == array_dim else idx for dd, idx in enumerate(x_part.shape)],
+        x_part.dtype,
+    )
+    inter = d_next = x_part
+    g_now = lax.dynamic_update_slice_in_dim(f_now, x_part, y1 * outer, axis=array_dim)
+    for it in range(1, spare // 2 + 1):
+        f_next = range(spare)
+        now = map(lambda dd: (dd, (dd + 1) % spare), f_next)
+        a_now = list(now)
+        inter = lax.ppermute(inter, link_axis, a_now)
+        g_now = lax.dynamic_update_slice_in_dim(
+            g_now, inter, (y1 - it) % spare * outer, axis=array_dim
+        )
+        if 2 * it < spare:
+            vec_out = list(map(lambda dd: (dd, (dd - 1) % spare), range(spare)))
+            d_next = lax.ppermute(d_next, link_axis, vec_out)
+            g_now = lax.dynamic_update_slice_in_dim(
+                g_now, d_next, (y1 + it) % spare * outer, axis=array_dim
+            )
+    return g_now
+
+
 def shards(hidden, routes, route_weights, pre_gain, out_gain, gate_weight, up_weight, down_weight):
     row_count, col_part = hidden.shape
     tp_count = lax.axis_size("tp")
@@ -16,7 +43,7 @@
     copies = req_count // E
     slot_count = CAP // copies
     stream = hidden.astype(jnp.float32)
-    whole_rows = lax.all_gather(hidden, "tp", axis=1, tiled=True).astype(jnp.float32)
+    whole_rows = bring_space(hidden, 1).astype(jnp.float32)
     meansq = jnp.sum(whole_rows * whole_rows, axis=1) / full_width
     normed_in = (whole_rows * lax.rsqrt(meansq + epsilon)[:, None] * pre_gain[None, :]).astype(
         jnp.bfloat16

time: 218 us -> 205 us (0.940)
  waiting for transfers between devices: 85.7 us -> 68.8 us
  starting transfers between devices: 7.49 us -> 11.1 us
    all_gather x1 -> x0, waiting for transfers between devices: 24.6 us -> none  [shards(): lax.all_gather(hidden, 'tp', axis=1, tiled=True).astype(jnp.float32)]
    ppermute x0 -> x3, waiting for transfers between devices: none -> 9.82 us  [the longest x2 9.82 us: bring_space(): inter = lax.ppermute(inter, link_axis, a_now)]
    ppermute x0 -> x3, starting transfers between devices: none -> 3.61 us  [the longest x2 2.03 us: bring_space(): inter = lax.ppermute(inter, link_axis, a_now)]
  transfers between devices with their start and end apart: 3 -> 5, of which waited for: 3 -> 4; matrix products, arithmetic and copies ran while one was open for 2% -> 2% of each run, Pallas kernels for 0% -> 0%
where the time goes in v1:
time: 205 us
  waiting for transfers between devices  68.8 us (34%)
  blocking collectives  66.9 us (33%)
  matrix products  31.4 us (15%)
  between operations  14.3 us (7%)
  starting transfers between devices  11.1 us (5%)
  local copies, waits for them, and re-layouts  7.7 us (4%)
  other arithmetic  4.67 us (2%)
    all_to_all x1, blocking collectives, shards(): lax.all_to_all(outgoing, 'req', split_axis=0, concat_axis=0, tiled=True)  58.4 us
    reduce_scatter x1, waiting for transfers between devices, shards(): lax.psum_scatter(partial_out.reshape(sources, items, widths).astype(jnp.b...  42.7 us
    dot_general x1, matrix products, shards(): jnp.dot(activ, down_weight[0], preferred_element_type=jnp.float32)  20.6 us
    all_to_all x1, waiting for transfers between devices, shards(): lax.all_to_all(summed, 'req', split_axis=0, concat_axis=0, tiled=True)  16.3 us
    ppermute x2, waiting for transfers between devices, bring_space(): inter = lax.ppermute(inter, link_axis, a_now)  9.82 us
    psum x1, blocking collectives, shards(): out_sums = lax.psum(jnp.sum(total_stream * total_stream, axis=1), 'tp')  8.56 us
    dot_general x1, matrix products, shards(): jnp.dot(flat_rows, gate_weight[0], preferred_element_type=jnp.float32)  8.45 us
    all_to_all x1, starting transfers between devices, shards(): lax.all_to_all(summed, 'req', split_axis=0, concat_axis=0, tiled=True)  7.41 us
  transfers between devices with their start and end apart: 5, of which 4 were waited for; matrix products, arithmetic and copies ran while one was open for 2% of the time, Pallas kernels for 0%

profile of v1, /device:TPU:0, one launch (start us, length us, event | category | flops | bytes accessed | tf_op | source)
XLA Modules:
  0.0 204.8 jit_solution(2388450022076485013)
XLA Ops:
  7.2 0.0 reduce-scatter.2.cloned.1.call-start
  7.2 1.7 collective-permute-start
  8.9 1.6 collective-permute-start.1
  10.5 0.8 copy.27
  11.3 0.1 eq.66
  11.5 0.1 eq.62
  11.6 1.1 reduce-window.6
  12.8 0.2 slice_reduce_fusion
  13.0 0.1 fusion.27
  13.1 0.1 reduce_sum.41
  13.3 0.1 copy.29
  13.4 0.7 fusion.31
  14.1 2.8 %collective-permute-done = bf16[256,512]{1,0:T(8,128)(2,1)S(1)} collective-permute-done((bf16[256,512]{1,0:T(8,128)(2,1)}, bf16[256,512]{1,0:T(8,128)(2,1)S(1)}, u32[]{:S(2)}, u32[]{:S(2)}) %collective-permute-start) | collective-permute-done | bytes 262176 | tf_op jit(solution)/shard_map/ppermute | solution.py:25
  16.9 0.3 collective-permute-start.2
  17.2 0.1 broadcast_in_dim.2
  17.3 1.0 constant_dynamic-update-slice_fusion.3
  18.4 0.0 collective-permute-done.1
  18.4 7.0 %collective-permute-done.2 = bf16[256,512]{1,0:T(8,128)(2,1)S(1)} collective-permute-done((bf16[256,512]{1,0:T(8,128)(2,1)S(1)}, bf16[256,512]{1,0:T(8,128)(2,1)S(1)}, u32[]{:S(2)}, u32[]{:S(2)}) %collective-permute-start.2) | collective-permute-done | bytes 262176 | tf_op jit(solution)/shard_map/ppermute | solution.py:25
  25.5 0.0 slice-start
  25.5 0.3 fusion.16
  25.8 0.0 slice-start.1
  25.8 2.3 %convolution_convert_fusion = bf16[1024,2048]{1,0:T(8,128)(2,1)S(1)} fusion(bf16[256,2048]{1,0:T(8,128)(2,1)S(1)} %constant_dynamic-update-slice_fusion, f32[2048]{0:T(1024)} %param.11, f32[256]{0:T(256)S(1)} %add_rsqrt_fusion.1, s32[256]{0:T(256)S(1)} %bitcast.40, s32[256]{0:T(256)S(1)} %bitcast.39), kind=kOutput, calls=%fused_computation.8 | convolution fusion | flops 1078722560 | bytes 5254144 | tf_op jit(solution)/shard_map/dot_general | solution.py:63
  28.1 58.4 %all_to_all.10 = bf16[32,32,2048]{2,1,0:T(8,128)(2,1)S(1)} all-to-all(bf16[32,32,2048]{2,1,0:T(8,128)(2,1)S(1)} %bitcast.33), channel_id=1, replica_groups=mesh['req'=32,'tp'=4] {'req'}, dimensions={0} | all-to-all | bytes 8388608 | tf_op jit(solution)/shard_map/all_to_all | solution.py:67
  86.5 0.0 copy-start
  86.5 2.1 %copy-done = bf16[32,32,2048]{2,1,0:T(8,128)(2,1)} copy-done((bf16[32,32,2048]{2,1,0:T(8,128)(2,1)}, bf16[32,32,2048]{2,1,0:T(8,128)(2,1)S(1)}, u32[]{:S(2)}) %copy-start) | copy-done | bytes 4194328
  88.5 0.0 slice-done
  88.5 0.0 slice-done.1
  88.5 8.5 %fusion.4 = f32[1024,1408]{1,0:T(8,128)} fusion(bf16[1024,2048]{1,0:T(8,128)(2,1)S(1)} %bitcast.36, bf16[1,2048,1408]{2,1,0:T(8,128)(2,1)S(1)} %bitcast.43), kind=kOutput, calls=%fused_computation.5 | convolution fusion | flops 5905580032 | bytes 15728640 | tf_op jit(solution)/shard_map/dot_general | solution.py:70
  97.0 20.6 %fusion.10 = bf16[1024,2048]{1,0:T(8,128)(2,1)} fusion(bf16[1,1408,2048]{2,1,0:T(8,128)(2,1)} %param.15, f32[1024,1408]{1,0:T(8,128)} %fusion.4, bf16[1024,2048]{1,0:T(8,128)(2,1)} %bitcast.37, bf16[1,2048,1408]{2,1,0:T(8,128)(2,1)} %param.14), kind=kOutput, calls=%fused_computation.9 | convolution fusion | flops 11821907968 | bytes 25690112 | tf_op jit(solution)/shard_map/dot_general | solution.py:73
  117.6 0.0 copy-start.2
  117.6 0.0 reduce-scatter.2.cloned.1.call-update
  117.7 0.0 copy-start.1
  117.7 0.0 copy-start.3
  117.7 42.7 %reduce-scatter.2.cloned.1.call-done = bf16[32,32,512]{2,1,0:T(8,128)(2,1)} async-done(((bf16[32,32,2048]{2,1,0:T(8,128)(2,1)}), bf16[32,32,512]{2,1,0:T(8,128)(2,1)}) %reduce-scatter.2.cloned.1.call-update) | async-done | bytes 1048592 | tf_op jit(solution)/shard_map/reduce_scatter | solution.py:75
  160.4 7.4 %all-to-all-start.1 = ((bf16[32,32,512]{2,1,0:T(8,128)(2,1)}), bf16[32,32,512]{2,1,0:T(8,128)(2,1)S(1)}, u32[]{:S(2)}, u32[]{:S(2)}) async-start(bf16[32,32,512]{2,1,0:T(8,128)(2,1)} %reduce-scatter.2.cloned.1.call-done), calls=%async_computation.2 | async-start | bytes 2097152 | tf_op jit(solution)/shard_map/all_to_all | solution.py:81
  167.8 0.1 reshape.153
  167.9 0.0 copy-done.2
  167.9 0.1 copy.34
  168.1 16.3 %all-to-all-done.1 = bf16[32,32,512]{2,1,0:T(8,128)(2,1)S(1)} async-done(((bf16[32,32,512]{2,1,0:T(8,128)(2,1)}), bf16[32,32,512]{2,1,0:T(8,128)(2,1)S(1)}, u32[]{:S(2)}, u32[]{:S(2)}) %all-to-all-start.1) | async-done | bytes 1048608 | tf_op jit(solution)/shard_map/all_to_all | solution.py:81
  184.4 2.0 gather_fusion
  186.4 0.7 reshape.154
  187.0 1.3 multiply_reduce_fusion
  188.4 0.0 copy-done.1
  188.4 0.2 multiply_reduce_fusion.1
  188.6 8.6 %psum.7 = f32[256]{0:T(256)S(1)} all-reduce(f32[256]{0:T(256)S(1)} %multiply_reduce_fusion.1), channel_id=1, replica_groups=mesh['req'=32,'tp'=4] {'tp'}, use_global_device_ids=true, to_apply=%region_7.8 | all-reduce | flops 256 | bytes 2048 | tf_op jit(solution)/shard_map/psum | solution.py:86
  197.1 0.0 copy-done.3
  197.1 0.9 multiply_convert_fusion.1
  (12 shorter events, 0.2 us)
Async XLA Ops:
  7.2 153.2 %reduce-scatter.2.cloned.1.call-start = ((), (), s32[]{:S(2)}) async-start(), calls=%async_computation.3 | async-start | bytes 5242880 | tf_op jit(solution)/shard_map/reduce_scatter | solution.py:75
  7.2 9.7 %collective-permute-start = (bf16[256,512]{1,0:T(8,128)(2,1)}, bf16[256,512]{1,0:T(8,128)(2,1)S(1)}, u32[]{:S(2)}, u32[]{:S(2)}) collective-permute-start(bf16[256,512]{1,0:T(8,128)(2,1)} %param.8), channel_id=1, source_target_pairs={{0,1},{1,2},{2,3},{3,0},{4,5},{5,6},{6,7},{7,4},{8,9},{9,10},{10,1... | collective-permute-start | bytes 786440 | tf_op jit(solution)/shard_map/ppermute | solution.py:25
  8.9 9.5 %collective-permute-start.1 = (bf16[256,512]{1,0:T(8,128)(2,1)}, bf16[256,512]{1,0:T(8,128)(2,1)S(1)}, u32[]{:S(2)}, u32[]{:S(2)}) collective-permute-start(bf16[256,512]{1,0:T(8,128)(2,1)} %param.8), channel_id=1, source_target_pairs={{0,3},{1,0},{2,1},{3,2},{4,7},{5,4},{6,5},{7,6},{8,11},{9,8},{10,9... | collective-permute-start | bytes 786440 | tf_op jit(solution)/shard_map/ppermute | solution.py:31
  16.9 8.6 %collective-permute-start.2 = (bf16[256,512]{1,0:T(8,128)(2,1)S(1)}, bf16[256,512]{1,0:T(8,128)(2,1)S(1)}, u32[]{:S(2)}, u32[]{:S(2)}) collective-permute-start(bf16[256,512]{1,0:T(8,128)(2,1)S(1)} %collective-permute-done), channel_id=1, source_target_pairs={{0,1},{1,2},{2,3},{3,0},{4,5},{5,6},{6,7},{7,4},{8,9},{9,10},{10,1... | collective-permute-start | bytes 786440 | tf_op jit(solution)/shard_map/ppermute | solution.py:25
  25.5 63.1 %slice-start = ((s8[5767168]{0:T(1024)(128)(4,1)}), s8[4194304]{0:T(1024)(128)(4,1)S(1)}, s32[]{:S(2)}) async-start(s8[5767168]{0:T(1024)(128)(4,1)} %bitcast.42), calls=%async_computation.4 | async-start | bytes 8388608
  25.8 62.7 %slice-start.1 = ((s8[5767168]{0:T(1024)(128)(4,1)}), s8[1572864]{0:T(1024)(128)(4,1)S(1)}, s32[]{:S(2)}) async-start(s8[5767168]{0:T(1024)(128)(4,1)} %bitcast.42), calls=%async_computation.5 | async-start | bytes 3145728
  86.5 2.1 %copy-start = (bf16[32,32,2048]{2,1,0:T(8,128)(2,1)}, bf16[32,32,2048]{2,1,0:T(8,128)(2,1)S(1)}, u32[]{:S(2)}) copy-start(bf16[32,32,2048]{2,1,0:T(8,128)(2,1)S(1)} %all_to_all.10) | copy-start | bytes 12582916
  117.6 50.3 %copy-start.2 = (f32[256,2]{0,1:T(2,128)S(1)}, f32[256,2]{0,1:T(2,128)}, u32[]{:S(2)}) copy-start(f32[256,2]{0,1:T(2,128)} %param.10) | copy-start | bytes 6148
  117.7 70.7 %copy-start.1 = (bf16[256,512]{1,0:T(8,128)(2,1)S(1)}, bf16[256,512]{1,0:T(8,128)(2,1)}, u32[]{:S(2)}) copy-start(bf16[256,512]{1,0:T(8,128)(2,1)} %param.8) | copy-start | bytes 786436
  117.7 79.5 %copy-start.3 = (f32[512]{0:T(512)S(1)}, f32[512]{0:T(512)}, u32[]{:S(2)}) copy-start(f32[512]{0:T(512)} %param.12) | copy-start | bytes 6148
  160.4 24.0 %all-to-all-start.1 = ((bf16[32,32,512]{2,1,0:T(8,128)(2,1)}), bf16[32,32,512]{2,1,0:T(8,128)(2,1)S(1)}, u32[]{:S(2)}, u32[]{:S(2)}) async-start(bf16[32,32,512]{2,1,0:T(8,128)(2,1)} %reduce-scatter.2.cloned.1.call-done), calls=%async_computation.2 | async-start | bytes 2097152 | tf_op jit(solution)/shard_map/all_to_all | solution.py:81
Sparse Core Ops, SparseCore 0:
  117.8 42.5 reduce-scatter.1
